TPU v7x, 32 devices: a whole 2x2x4 slice. The times are simulated.
32 devices in a mesh: seq: 4 (over y, x), tp: 8 (over z, core).
Axes of the slice: x: 2, y: 2, z: 4, core: 2. Of those that a mesh axis runs over, the one named last changes fastest.
Arguments:
- hidden: bfloat16 [512, 28672], P('seq', 'tp'), may hold values from -6 to 6
- down_weight: bfloat16 [28672, 8192], P('tp', 'seq'), may hold values from -0.03125 to 0.03125
- channel_scale: float32 [8192], P('seq'), may hold values from 0.25 to 1.75
Outputs:
- mixed: bfloat16 [512, 8192], P('tp', 'seq')
All inputs are finite; a program needn't handle non-finite values.
Results may differ from a plain program's by a relative error of at most 0.0049.
Values may be sent and summed in bfloat16 or wider, within the bound.
No kernel may reach another device: no remote copies, remote signals or barrier semaphores. Data moves between devices by JAX's collectives and lax.ppermute only.
A program may use at most 128 MiB of HBM per device.

v0:
```python
import math
import jax
import jax.numpy as jnp
import numpy as np
from jax import lax
from jax.sharding import PartitionSpec as P

PALEY = 28


def paley_table():
    residues = set((value * value % 13 for value in range(1, 13)))
    conference = np.zeros((14, 14))
    conference[0, 1:] = 1.0
    conference[1:, 0] = 1.0
    for first in range(13):
        for second in range(13):
            gap = (second - first) % 13
            if gap != 0:
                conference[1 + first, 1 + second] = 1.0 if gap in residues else -1.0
    upper = np.array([[1.0, 1.0], [1.0, -1.0]])
    lower = np.array([[1.0, -1.0], [-1.0, -1.0]])
    return np.kron(conference, upper) + np.kron(np.eye(14), lower)


def walsh_table(order):
    index_rows = np.arange(order)[:, None]
    index_cols = np.arange(order)[None, :]
    signs = np.ones((order, order))
    bit_value = 1
    while bit_value < order:
        both_set = index_rows // bit_value % 2 * (index_cols // bit_value % 2)
        signs = signs * (1 - 2 * both_set)
        bit_value = bit_value * 2
    return signs


def shards(hidden, down_weight, channel_scale):
    tp_count = lax.axis_size("tp")
    units = hidden.shape[1]
    total_units = units * tp_count
    local_table = jnp.asarray(np.kron(walsh_table(units // PALEY), paley_table()), jnp.bfloat16)
    factor = 1.0 / math.sqrt(total_units)
    spread = lax.all_to_all(hidden, "tp", split_axis=0, concat_axis=1, tiled=True)
    few_rows = spread.shape[0]
    blocks = spread.reshape(few_rows, tp_count, units)
    inner = jnp.einsum("rtl,lm->rtm", blocks, local_table, preferred_element_type=jnp.float32)
    cross_table = jnp.asarray(walsh_table(tp_count), jnp.float32)
    outer = jnp.einsum("rtm,tu->rum", inner, cross_table, precision=lax.Precision.HIGHEST)
    turned = (outer * factor).astype(jnp.bfloat16).reshape(few_rows, total_units)
    rotated = lax.all_to_all(turned, "tp", split_axis=1, concat_axis=0, tiled=True)
    partial_terms = jnp.dot(
        lax.all_gather(rotated, "seq", axis=0, tiled=True),
        down_weight,
        preferred_element_type=jnp.float32,
    )
    summed = lax.psum_scatter(partial_terms, "tp", scatter_dimension=0, tiled=True)
    return (summed * channel_scale[None, :]).astype(jnp.bfloat16)


def solution(mesh):
    placed = (P("seq", "tp"), P("tp", "seq"), P("seq"))
    return jax.shard_map(
        shards, mesh=mesh, in_specs=placed, out_specs=P("tp", "seq"), check_vma=False
    )
```

profile of v0, /device:TPU:0, one launch (start us, length us, event | category | flops | bytes accessed | tf_op | source)
XLA Modules:
  0.0 195.8 jit_solution(9701736656185318527)
XLA Ops:
  6.5 0.0 all-gather.2.cloned.1.call-start
  6.5 30.1 %all_to_all.32 = bf16[8,16,3584]{2,1,0:T(8,128)(2,1)S(1)} all-to-all(bf16[8,16,3584]{2,1,0:T(8,128)(2,1)} %bitcast.19), channel_id=1, replica_groups=mesh['seq'=4,'tp'=8] {'tp'}, dimensions={0} | all-to-all | bytes 1835008 | tf_op jit(solution)/shard_map/all_to_all | solution.py:44
  36.6 0.0 copy-start.1
  36.6 10.7 %convolution_bitcast_fusion = f32[16,8,3584]{2,1,0:T(8,128)S(1)} fusion(bf16[3584,3584,1]{1,0,2:T(8,128)(2,1)} %constant.8, bf16[8,16,3584]{2,1,0:T(8,128)(2,1)S(1)} %all_to_all.32), kind=kOutput, calls=%fused_computation.1 | convolution fusion | flops 3288334336 | bytes 28442624 | tf_op jit(solution)/shard_map/rtl,lm->rtm/dot_general | solution.py:47
  47.3 0.0 copy-done.1
  47.3 1.7 fusion.1
  49.0 0.3 copy.11
  49.3 26.9 %all_to_all.33 = bf16[16,8,3584]{2,0,1:T(8,128)(2,1)} all-to-all(bf16[16,8,3584]{2,0,1:T(8,128)(2,1)S(1)} %copy.11), channel_id=1, replica_groups=mesh['seq'=4,'tp'=8] {'tp'}, dimensions={1} | all-to-all | bytes 1835008 | tf_op jit(solution)/shard_map/all_to_all | solution.py:51
  76.2 0.0 all-gather.2.cloned.1.call-update
  76.2 0.0 reduce-scatter.2.cloned.1.call-start
  76.2 47.4 %all-gather.2.cloned.1.call-done = bf16[512,3584]{1,0:T(8,128)(2,1)} async-done(((bf16[128,3584]{1,0:T(8,128)(2,1)}), bf16[512,3584]{1,0:T(8,128)(2,1)}) %all-gather.2.cloned.1.call-update) | async-done | bytes 3670032 | tf_op jit(solution)/shard_map/all_gather | solution.py:53
  123.6 13.4 %fusion.2 = f32[512,2048]{1,0:T(8,128)} fusion(bf16[512,3584]{1,0:T(8,128)(2,1)} %all-gather.2.cloned.1.call-done, bf16[3584,2048]{1,0:T(8,128)(2,1)} %param.6), kind=kOutput, calls=%fused_computation.6 | convolution fusion | flops 7516192768 | bytes 22544384 | tf_op jit(solution)/shard_map/dot_general | solution.py:52
  137.0 0.0 copy-start
  137.0 0.0 reduce-scatter.2.cloned.1.call-update
  137.0 50.2 %reduce-scatter.2.cloned.1.call-done = f32[64,2048]{1,0:T(8,128)} async-done(((f32[512,2048]{1,0:T(8,128)}), f32[64,2048]{1,0:T(8,128)}) %reduce-scatter.2.cloned.1.call-update) | async-done | bytes 524304 | tf_op jit(solution)/shard_map/reduce_scatter | solution.py:57
  187.2 0.0 copy-done
  187.2 1.8 multiply_convert_fusion
Async XLA Ops:
  6.5 117.1 %all-gather.2.cloned.1.call-start = ((), (), s32[]{:S(2)}) async-start(), calls=%async_computation.3 | async-start | bytes 4587520 | tf_op jit(solution)/shard_map/all_gather | solution.py:53
  36.6 10.7 %copy-start.1 = (f32[8,8,1]{0,1,2:T(8,128)S(1)}, f32[8,8,1]{0,1,2:T(8,128)}, u32[]{:S(2)}) copy-start(f32[8,8,1]{0,1,2:T(8,128)} %constant.9) | copy-start | bytes 772
  76.2 111.0 %reduce-scatter.2.cloned.1.call-start = ((), (), s32[]{:S(2)}) async-start(), calls=%async_computation.4 | async-start | bytes 4718592 | tf_op jit(solution)/shard_map/reduce_scatter | solution.py:57
  137.0 50.2 %copy-start = (f32[2048]{0:T(1024)S(1)}, f32[2048]{0:T(1024)}, u32[]{:S(2)}) copy-start(f32[2048]{0:T(1024)} %param.7) | copy-start | bytes 24580
Sparse Core Ops, SparseCore 0:
  76.3 47.2 all-gather.1
  137.1 49.9 reduce-scatter.1
where the time goes:
time: 196 us
  waiting for transfers between devices  97.6 us (50%)
  blocking collectives  57 us (29%)
  matrix products  25.7 us (13%)
  between operations  13.4 us (7%)
    reduce_scatter x1, waiting for transfers between devices, shards(): lax.psum_scatter(partial_terms, 'tp', scatter_dimension=0, tiled=True)  50.2 us
    all_gather x1, waiting for transfers between devices, shards(): lax.all_gather(rotated, 'seq', axis=0, tiled=True)  47.4 us
    all_to_all x1, blocking collectives, shards(): lax.all_to_all(hidden, 'tp', split_axis=0, concat_axis=1, tiled=True)  30.1 us
    all_to_all x1, blocking collectives, shards(): lax.all_to_all(turned, 'tp', split_axis=1, concat_axis=0, tiled=True)  26.9 us
    dot_general x1, matrix products, shards(): jnp.dot(lax.all_gather(rotated, 'seq', axis=0, tiled=True), down_weight,...  13.4 us
    dot_general x1, matrix products, shards(): jnp.einsum('rtl,lm->rtm', blocks, local_table, preferred_element_type=jnp...  10.7 us
  transfers between devices with their start and end apart: 2, of which 2 were waited for; matrix products, arithmetic and copies ran while one was open for 0% of the time, Pallas kernels for 0%

commit v1 on v0

--- a/solution.py
+++ b/solution.py
@@ -41,7 +41,10 @@
     total_units = units * tp_count
     local_table = jnp.asarray(np.kron(walsh_table(units // PALEY), paley_table()), jnp.bfloat16)
     factor = 1.0 / math.sqrt(total_units)
-    spread = lax.all_to_all(hidden, "tp", split_axis=0, concat_axis=1, tiled=True)
+    spread = jnp.concatenate(
+        lax.all_to_all(jnp.stack(jnp.split(hidden, lax.axis_size("tp"), axis=0)), "tp", 0, 0),
+        axis=1,
+    )
     few_rows = spread.shape[0]
     blocks = spread.reshape(few_rows, tp_count, units)
     inner = jnp.einsum("rtl,lm->rtm", blocks, local_table, preferred_element_type=jnp.float32)

time: 196 us -> 203 us (1.036)
  local copies, waits for them, and re-layouts: 0.28 us -> 7.52 us
    unnamed x4 -> x11, local copies, waits for them, and re-layouts: 0.01 us -> 6.35 us
where the time goes in v1:
time: 203 us
  waiting for transfers between devices  97.5 us (48%)
  blocking collectives  56.8 us (28%)
  matrix products  25.6 us (13%)
  between operations  13.4 us (7%)
  local copies, waits for them, and re-layouts  7.52 us (4%)
    reduce_scatter x1, waiting for transfers between devices, shards(): lax.psum_scatter(partial_terms, 'tp', scatter_dimension=0, tiled=True)  50.2 us
    all_gather x1, waiting for transfers between devices, shards(): lax.all_gather(rotated, 'seq', axis=0, tiled=True)  47.3 us
    all_to_all x1, blocking collectives, shards(): lax.all_to_all(jnp.stack(jnp.split(hidden, lax.axis_size('tp'), axis=0)),...  29.9 us
    all_to_all x1, blocking collectives, shards(): lax.all_to_all(turned, 'tp', split_axis=1, concat_axis=0, tiled=True)  26.9 us
    dot_general x1, matrix products, shards(): jnp.dot(lax.all_gather(rotated, 'seq', axis=0, tiled=True), down_weight,...  13.4 us
    dot_general x1, matrix products, shards(): jnp.einsum('rtl,lm->rtm', blocks, local_table, preferred_element_type=jnp...  10.6 us
    unnamed x11, local copies, waits for them, and re-layouts  6.35 us
  transfers between devices with their start and end apart: 2, of which 2 were waited for; matrix products, arithmetic and copies ran while one was open for 0% of the time, Pallas kernels for 0%

profile of v1, /device:TPU:0, one launch (start us, length us, event | category | flops | bytes accessed | tf_op | source)
XLA Modules:
  0.0 202.8 jit_solution(11129231996708976126)
XLA Ops:
  6.5 0.0 all-gather.2.cloned.1.call-start
  6.5 0.9 bitcast_dynamic-update-slice_fusion.7
  7.4 0.9 bitcast_dynamic-update-slice_fusion.6
  8.3 0.9 bitcast_dynamic-update-slice_fusion.5
  9.3 0.9 bitcast_dynamic-update-slice_fusion.4
  10.2 0.9 bitcast_dynamic-update-slice_fusion.3
  11.1 0.9 bitcast_dynamic-update-slice_fusion.2
  12.0 0.9 bitcast_dynamic-update-slice_fusion.1
  12.9 0.9 bitcast_dynamic-update-slice_fusion
  13.8 29.9 %all_to_all.21 = bf16[8,16,3584]{2,1,0:T(8,128)(2,1)S(1)} all-to-all(bf16[8,16,3584]{2,1,0:T(8,128)(2,1)S(1)} %bitcast_dynamic-update-slice_fusion), channel_id=1, replica_groups=mesh['seq'=4,'tp'=8] {'tp'}, dimensions={0} | all-to-all | bytes 1835008 | tf_op jit(solution)/shard_map/all_to_all | solution.py:45
  43.7 0.0 copy-start.1
  43.7 10.6 %fusion.2 = f32[16,8,3584]{2,1,0:T(8,128)S(1)} fusion(bf16[3584,3584,1]{1,0,2:T(8,128)(2,1)} %constant.8, bf16[8,16,3584]{2,1,0:T(8,128)(2,1)S(1)} %all_to_all.21), kind=kOutput, calls=%fused_computation.4 | convolution fusion | flops 3288334336 | bytes 28442624 | tf_op jit(solution)/shard_map/rtl,lm->rtm/dot_general | solution.py:50
  54.3 0.0 copy-done.1
  54.3 1.7 fusion.1
  56.0 0.3 copy.18
  56.2 26.9 %all_to_all.22 = bf16[16,8,3584]{2,0,1:T(8,128)(2,1)} all-to-all(bf16[16,8,3584]{2,0,1:T(8,128)(2,1)S(1)} %copy.18), channel_id=1, replica_groups=mesh['seq'=4,'tp'=8] {'tp'}, dimensions={1} | all-to-all | bytes 1835008 | tf_op jit(solution)/shard_map/all_to_all | solution.py:54
  83.1 0.0 all-gather.2.cloned.1.call-update
  83.2 0.0 reduce-scatter.2.cloned.1.call-start
  83.2 47.3 %all-gather.2.cloned.1.call-done = bf16[512,3584]{1,0:T(8,128)(2,1)} async-done(((bf16[128,3584]{1,0:T(8,128)(2,1)}), bf16[512,3584]{1,0:T(8,128)(2,1)}) %all-gather.2.cloned.1.call-update) | async-done | bytes 3670032 | tf_op jit(solution)/shard_map/all_gather | solution.py:56
  130.6 13.4 %fusion.3 = f32[512,2048]{1,0:T(8,128)} fusion(bf16[512,3584]{1,0:T(8,128)(2,1)} %all-gather.2.cloned.1.call-done, bf16[3584,2048]{1,0:T(8,128)(2,1)} %param.6), kind=kOutput, calls=%fused_computation.14 | convolution fusion | flops 7516192768 | bytes 22544384 | tf_op jit(solution)/shard_map/dot_general | solution.py:55
  143.9 0.0 reduce-scatter.2.cloned.1.call-update
  144.0 50.2 %reduce-scatter.2.cloned.1.call-done = f32[64,2048]{1,0:T(8,128)} async-done(((f32[512,2048]{1,0:T(8,128)}), f32[64,2048]{1,0:T(8,128)}) %reduce-scatter.2.cloned.1.call-update) | async-done | bytes 524304 | tf_op jit(solution)/shard_map/reduce_scatter | solution.py:60
  194.1 0.0 copy-done
  194.1 1.8 multiply_convert_fusion
  (1 shorter events, 0.0 us)
Async XLA Ops:
  6.5 124.0 %all-gather.2.cloned.1.call-start = ((), (), s32[]{:S(2)}) async-start(), calls=%async_computation.3 | async-start | bytes 4587520 | tf_op jit(solution)/shard_map/all_gather | solution.py:56
  43.7 10.6 %copy-start.1 = (f32[8,8,1]{0,1,2:T(8,128)S(1)}, f32[8,8,1]{0,1,2:T(8,128)}, u32[]{:S(2)}) copy-start(f32[8,8,1]{0,1,2:T(8,128)} %constant.9) | copy-start | bytes 772
  83.2 111.0 %reduce-scatter.2.cloned.1.call-start = ((), (), s32[]{:S(2)}) async-start(), calls=%async_computation.4 | async-start | bytes 4718592 | tf_op jit(solution)/shard_map/reduce_scatter | solution.py:60
  143.9 50.2 %copy-start = (f32[2048]{0:T(1024)S(1)}, f32[2048]{0:T(1024)}, u32[]{:S(2)}) copy-start(f32[2048]{0:T(1024)} %param.7) | copy-start | bytes 24580
Sparse Core Ops, SparseCore 0:
  83.3 47.2 all-gather.1
  144.1 49.9 reduce-scatter.1
